TPU v7x, 32 devices: a whole 2x2x4 slice. The times are simulated.
32 devices in a mesh: obs: 16 (over z, x, core), freq: 2 (over y).
Axes of the slice: x: 2, y: 2, z: 4, core: 2. Of those that a mesh axis runs over, the one named last changes fastest.
Arguments:
- cell_spectra: bfloat16 [8192, 512], P('obs', 'freq'), may hold values from -6 to 6
- cell_weight: float32 [8192], P('obs'), may hold values from 0.25 to 1
- cell_owner: int32 [8192, 1], P('obs'), may hold values from 0 to 15; in each aligned block of 512 rows (0 to 511, 512 to 1023, ...) at most 80 rows name the same one
- cell_local: int32 [8192], P('obs'), may hold values from 0 to 31
- panel_position: float32 [3, 512], replicated, may hold values from -8 to 8
- observer_position: float32 [3, 1024], P(None, 'obs'), may hold values from -40 to 40, as said below
Outputs:
- pressure: float32 [64, 2, 1024], P('freq', None, 'obs')
- level: float32 [1024], P('obs')
Inputs may be any that keep to these rules, and one draw needn't show every extreme that they name: `cell_owner`: among the 512 cells of one partition at most 80 name one panel group, and in every draw some partition sends exactly 80 cells to one group. `observer_position`: every observer lies between 20 and 40 from the anchor (0, 0, 0).
All inputs are finite; a program needn't handle non-finite values.
Results may differ from a plain program's by a relative error of at most 0.0029.
Values may be sent and summed in bfloat16 or wider, within the bound.
No kernel may reach another device: no remote copies, remote signals or barrier semaphores. Data moves between devices by JAX's collectives and lax.ppermute only.
A program may use at most 64 MiB of HBM per device.

v0:
```python
import math
import jax
import jax.numpy as jnp
from jax import lax
from jax.sharding import PartitionSpec as P

wave_step = 0.1
reference_radius = 10.0


def phase_powers(distance, wave_numbers):
    needed = wave_numbers.shape[0]
    cosine = jnp.cos(wave_numbers[0] * distance)[None]
    sine = jnp.sin(wave_numbers[0] * distance)[None]
    step_cos = jnp.cos(wave_step * distance)[None]
    step_sin = jnp.sin(wave_step * distance)[None]
    while cosine.shape[0] < needed:
        later_cos = cosine * step_cos - sine * step_sin
        later_sin = sine * step_cos + cosine * step_sin
        cosine = jnp.concatenate([cosine, later_cos], axis=0)
        sine = jnp.concatenate([sine, later_sin], axis=0)
        step_cos, step_sin = (step_cos * step_cos - step_sin * step_sin, 2.0 * step_cos * step_sin)
    return (cosine, sine)


def kernel_block(source, panel_points, observer_points, wave_numbers):
    offsets = observer_points[:, None, :] - panel_points[:, :, None]
    distance = jnp.sqrt(offsets[0] * offsets[0] + offsets[1] * offsets[1] + offsets[2] * offsets[2])
    inverse = 1.0 / distance
    heading = offsets * inverse[None]
    channels = jnp.transpose(source, (2, 1, 0))
    dipole_real = (
        heading[0][None] * channels[2][:, :, None]
        + heading[1][None] * channels[4][:, :, None]
        + heading[2][None] * channels[6][:, :, None]
    )
    dipole_imag = (
        heading[0][None] * channels[3][:, :, None]
        + heading[1][None] * channels[5][:, :, None]
        + heading[2][None] * channels[7][:, :, None]
    )
    waves = wave_numbers[:, None, None]
    amp_real = channels[0][:, :, None] + dipole_real * inverse[None] - waves * dipole_imag
    amp_imag = channels[1][:, :, None] + dipole_imag * inverse[None] + waves * dipole_real
    cosine, sine = phase_powers(distance, wave_numbers)
    weight_real = cosine * inverse[None]
    weight_imag = sine * inverse[None]
    real_part = jnp.sum(weight_real * amp_real + weight_imag * amp_imag, axis=1)
    imag_part = jnp.sum(weight_real * amp_imag - weight_imag * amp_real, axis=1)
    return jnp.stack([real_part, imag_part], axis=1)


def shards(cell_spectra, cell_weight, cell_owner, cell_local, panel_position, observer_position):
    cell_rows, columns = cell_spectra.shape
    freqs_dev = columns // 8
    groups = lax.axis_size("obs")
    panel_total = panel_position.shape[1]
    panels_dev = panel_total // groups
    observers_dev = observer_position.shape[1]
    weighted = (cell_weight[:, None] * cell_spectra.astype(jnp.float32)).astype(jnp.bfloat16)
    panel_index = cell_owner[:, 0] * panels_dev + cell_local
    selector = (jnp.arange(panel_total, dtype=jnp.int32)[:, None] == panel_index[None, :]).astype(
        jnp.bfloat16
    )
    local_source = jnp.dot(selector, weighted, preferred_element_type=jnp.float32)
    group_first = lax.axis_index("freq") * freqs_dev
    wave_numbers = wave_step * (
        (group_first + jnp.arange(freqs_dev, dtype=jnp.int32)).astype(jnp.float32) + 1.0
    )
    start_value = jnp.zeros((freqs_dev, 2, observers_dev), jnp.float32)
    arrived = lax.all_to_all(
        local_source.reshape(groups, panels_dev, columns), "obs", 0, 0, tiled=True
    )
    own_source = jnp.sum(arrived, axis=0)
    portion = lax.all_to_all(
        jnp.broadcast_to(own_source[None], (groups, panels_dev, columns)), "obs", 0, 0, tiled=True
    ).reshape(panel_total, columns)
    rows_count = portion.shape[0]
    tile_rows = math.gcd(rows_count, 256)

    def advance(turn, accum):
        source = lax.dynamic_slice_in_dim(portion, turn * tile_rows, tile_rows, 0).reshape(
            tile_rows, freqs_dev, 8
        )
        points = lax.dynamic_slice_in_dim(panel_position, turn * tile_rows, tile_rows, 1)
        return accum + kernel_block(source, points, observer_position, wave_numbers)

    summed = lax.fori_loop(0, rows_count // tile_rows, advance, start_value)
    pressure = summed * (reference_radius / math.sqrt(panel_total))
    energy = jnp.sum(pressure[:, 0] * pressure[:, 0] + pressure[:, 1] * pressure[:, 1], axis=0)
    if lax.axis_size("freq") == 2:
        band_total = energy + lax.ppermute(energy, "freq", [(0, 1), (1, 0)])
    else:
        band_total = lax.psum(energy, "freq")
    level = jnp.log(band_total / (freqs_dev * lax.axis_size("freq")) + 1e-06)
    return (pressure, level)


def solution(mesh):
    in_specs = (P("obs", "freq"), P("obs"), P("obs", None), P("obs"), P(), P(None, "obs"))
    out_specs = (P("freq", None, "obs"), P("obs"))
    return jax.shard_map(shards, mesh=mesh, in_specs=in_specs, out_specs=out_specs, check_vma=False)
```

profile of v0, /device:TPU:0, one launch (start us, length us, event | category | flops | bytes accessed | tf_op | source)
XLA Modules:
  0.0 64.2 jit_solution(14932165219836297983)
XLA Ops:
  0.7 0.7 %broadcast_multiply_fusion.1 = s32[512,1]{0,1:T(1,128)S(1)} fusion(s32[512,1]{0,1:T(1,128)} %param.10), kind=kLoop, calls=%fused_computation.92 | loop fusion | flops 512 | bytes 4096 | tf_op jit(solution)/shard_map/mul | solution.py:61
  1.3 0.7 %add.278 = s32[512]{0:T(512)S(1)} add(s32[512]{0:T(512)S(1)} %bitcast.81, s32[512]{0:T(512)} %param.11) | non-fusion elementwise | flops 512 | bytes 6144 | tf_op jit(solution)/shard_map/add | solution.py:61
  2.0 1.4 %fusion.12 = f32[512,256]{1,0:T(8,128)S(1)} fusion(s32[512]{0:T(512)S(1)} %add.278, bf16[512,256]{1,0:T(8,128)(2,1)} %param.8, f32[512]{0:T(512)} %param.9), kind=kOutput, calls=%fused_computation.83 | convolution fusion | flops 134873088 | bytes 790528 | tf_op jit(solution)/shard_map/dot_general | solution.py:65
  3.4 21.6 %all_to_all.10 = f32[16,32,256]{2,1,0:T(8,128)S(1)} all-to-all(f32[16,32,256]{2,1,0:T(8,128)S(1)} %bitcast.78), channel_id=1, replica_groups=mesh['obs'=16,'freq'=2] {'obs'}, dimensions={0} | all-to-all | bytes 1048576 | tf_op jit(solution)/shard_map/all_to_all | solution.py:71
  25.1 0.8 %broadcast_in_dim.41 = f32[16,32,256]{2,1,0:T(8,128)} broadcast(f32[32,256]{1,0:T(8,128)S(1)} %reduce_sum.44), dimensions={1,2} | broadcast | bytes 557056 | tf_op jit(solution)/shard_map/broadcast_in_dim | solution.py:76
  25.9 4.1 %all-to-all-start.1 = ((f32[16,32,256]{2,1,0:T(8,128)}), f32[16,32,256]{2,1,0:T(8,128)S(1)}, u32[]{:S(2)}, u32[]{:S(2)}) async-start(f32[16,32,256]{2,1,0:T(8,128)} %broadcast_in_dim.41), calls=%async_computation.1 | async-start | bytes 1048576 | tf_op jit(solution)/shard_map/all_to_all | solution.py:75
  30.0 14.4 %all-to-all-done.1 = f32[16,32,256]{2,1,0:T(8,128)S(1)} async-done(((f32[16,32,256]{2,1,0:T(8,128)}), f32[16,32,256]{2,1,0:T(8,128)S(1)}, u32[]{:S(2)}, u32[]{:S(2)}) %all-to-all-start.1) | async-done | bytes 524320 | tf_op jit(solution)/shard_map/all_to_all | solution.py:75
  44.5 15.4 %while.14 = (s32[]{:T(128)}, f32[32,2,64]{2,0,1:T(8,128)S(1)}, f32[32]{0:T(128)S(1)}, f32[3,64]{1,0:T(4,128)S(1)}, f32[3,512]{1,0:T(4,128)S(1)}, /*index=5*/f32[...) while((s32[]{:T(128)}, f32[32,2,64]{2,0,1:T(8,128)S(1)}, f32[32]{0:T(128)S(1)}, ...), condition=%wide.region_4.0_spmd.clone, body=%wide.region_1.0_spmd.clone.sunk | while | flops 22880256 | bytes 33503556 | solution.py:88
  44.5 0.1 broadcast_subtract_fusion.2
  44.6 0.6 subtract_bitcast_fusion.2
  45.2 0.5 constant_dynamic-update-slice_fusion.25
  46.0 0.1 constant_dynamic-update-slice_fusion.33
  46.2 0.1 constant_dynamic-update-slice_fusion.28
  46.3 0.2 subtract_dynamic-update-slice_fusion.2
  46.6 1.3 %copy-done = f32[32,256,64]{1,2,0:T(8,128)} copy-done((f32[32,256,64]{1,2,0:T(8,128)}, f32[32,256,64]{1,2,0:T(8,128)S(1)}, u32[]{:S(2)}) %copy-start) | copy-done | bytes 2097176 | tf_op jit(solution)/shard_map/while
  47.9 0.1 copy.38
  48.1 0.2 fusion.24
  48.3 0.1 broadcast_multiply_fusion.3
  48.4 3.7 %add_reduce_fusion.2 = (f32[32,64]{1,0:T(8,128)S(1)}, f32[32,64]{1,0:T(8,128)S(1)}) fusion(f32[32,256,64]{1,2,0:T(8,128)S(1)} %get-tuple-element.339, f32[32,256,64]{1,2,0:T(8,128)} %copy-done, f32[32,256]{1,0:T(8,128)S(1)} %get-tuple-element.343, f32[32,256]{1,0:T(8,128)S(1)} %get-tuple-element.344, f32[32,256]{1,0:T(8,128)S(1)} %get-tuple-element.347, ...), kind=kLoop, calls=%fused_computation.1.clone.1 | loop fusion | flops 14675968 | bytes 4735104 | tf_op jit(solution)/shard_map/while/body/eval_jaxpr/reduce_sum | solution.py:48
  52.2 0.1 broadcast_subtract_fusion.2
  52.4 0.6 subtract_bitcast_fusion.2
  52.9 0.5 constant_dynamic-update-slice_fusion.25
  53.7 0.1 constant_dynamic-update-slice_fusion.33
  54.1 0.2 subtract_dynamic-update-slice_fusion.2
  54.3 1.3 %copy-done = f32[32,256,64]{1,2,0:T(8,128)} copy-done((f32[32,256,64]{1,2,0:T(8,128)}, f32[32,256,64]{1,2,0:T(8,128)S(1)}, u32[]{:S(2)}) %copy-start) | copy-done | bytes 2097176 | tf_op jit(solution)/shard_map/while
  55.7 0.1 copy.38
  55.8 0.2 fusion.24
  56.0 0.1 broadcast_multiply_fusion.3
  56.2 3.7 %add_reduce_fusion.2 = (f32[32,64]{1,0:T(8,128)S(1)}, f32[32,64]{1,0:T(8,128)S(1)}) fusion(f32[32,256,64]{1,2,0:T(8,128)S(1)} %get-tuple-element.339, f32[32,256,64]{1,2,0:T(8,128)} %copy-done, f32[32,256]{1,0:T(8,128)S(1)} %get-tuple-element.343, f32[32,256]{1,0:T(8,128)S(1)} %get-tuple-element.344, f32[32,256]{1,0:T(8,128)S(1)} %get-tuple-element.347, ...), kind=kLoop, calls=%fused_computation.1.clone.1 | loop fusion | flops 14675968 | bytes 4735104 | tf_op jit(solution)/shard_map/while/body/eval_jaxpr/reduce_sum | solution.py:48
  60.1 1.6 %collective-permute-start = (f32[64]{0:T(128)S(1)}, f32[64]{0:T(128)S(1)}, u32[]{:S(2)}, u32[]{:S(2)}) collective-permute-start(f32[64]{0:T(128)S(1)} %fusion.16), channel_id=1, source_target_pairs={{0,1},{1,0},{2,3},{3,2},{4,5},{5,4},{6,7},{7,6},{8,9},{9,8},{10,11... | collective-permute-start | bytes 776 | tf_op jit(solution)/shard_map/ppermute | solution.py:92
  61.6 2.0 %collective-permute-done = f32[64]{0:T(128)S(1)} collective-permute-done((f32[64]{0:T(128)S(1)}, f32[64]{0:T(128)S(1)}, u32[]{:S(2)}, u32[]{:S(2)}) %collective-permute-start) | collective-permute-done | bytes 288 | tf_op jit(solution)/shard_map/ppermute | solution.py:92
  63.7 0.5 add_log_fusion
  (48 shorter events, 1.2 us)
Async XLA Ops:
  0.6 43.9 %copy-start.3 = (f32[3,512]{1,0:T(4,128)S(1)}, f32[3,512]{1,0:T(4,128)}, u32[]{:S(2)}) copy-start(f32[3,512]{1,0:T(4,128)} %param.12) | copy-start | bytes 18436
  0.6 43.8 %copy-start.1 = (f32[3,64]{1,0:T(4,128)S(1)}, f32[3,64]{1,0:T(4,128)}, u32[]{:S(2)}) copy-start(f32[3,64]{1,0:T(4,128)} %param.13) | copy-start | bytes 2308
  25.9 18.6 %all-to-all-start.1 = ((f32[16,32,256]{2,1,0:T(8,128)}), f32[16,32,256]{2,1,0:T(8,128)S(1)}, u32[]{:S(2)}, u32[]{:S(2)}) async-start(f32[16,32,256]{2,1,0:T(8,128)} %broadcast_in_dim.41), calls=%async_computation.1 | async-start | bytes 1048576 | tf_op jit(solution)/shard_map/all_to_all | solution.py:75
  46.6 1.3 %copy-start = (f32[32,256,64]{1,2,0:T(8,128)}, f32[32,256,64]{1,2,0:T(8,128)S(1)}, u32[]{:S(2)}) copy-start(f32[32,256,64]{1,2,0:T(8,128)S(1)} %get-tuple-element.340) | copy-start | bytes 6291460 | tf_op jit(solution)/shard_map/while
  54.3 1.3 %copy-start = (f32[32,256,64]{1,2,0:T(8,128)}, f32[32,256,64]{1,2,0:T(8,128)S(1)}, u32[]{:S(2)}) copy-start(f32[32,256,64]{1,2,0:T(8,128)S(1)} %get-tuple-element.340) | copy-start | bytes 6291460 | tf_op jit(solution)/shard_map/while
  60.0 4.2 %copy-start.2 = (f32[32,2,64]{2,1,0:T(2,128)}, f32[32,2,64]{2,1,0:T(2,128)S(1)}, u32[]{:S(2)}) copy-start(f32[32,2,64]{2,1,0:T(2,128)S(1)} %copy_multiply_fusion) | copy-start | bytes 49156
  60.1 3.6 %collective-permute-start = (f32[64]{0:T(128)S(1)}, f32[64]{0:T(128)S(1)}, u32[]{:S(2)}, u32[]{:S(2)}) collective-permute-start(f32[64]{0:T(128)S(1)} %fusion.16), channel_id=1, source_target_pairs={{0,1},{1,0},{2,3},{3,2},{4,5},{5,4},{6,7},{7,6},{8,9},{9,8},{10,11... | collective-permute-start | bytes 776 | tf_op jit(solution)/shard_map/ppermute | solution.py:92
where the time goes:
time: 64.6 us; the launch traced here: 64.2 us
  blocking collectives  21.6 us (33%)
  waiting for transfers between devices  16.5 us (26%)
  other arithmetic  13.5 us (21%)
  starting transfers between devices  5.68 us (9%)
  local copies, waits for them, and re-layouts  4.35 us (7%)
  matrix products  1.36 us (2%)
  between operations  0.71 us (1%)
    all_to_all x1, blocking collectives, shards(): lax.all_to_all(local_source.reshape(groups, panels_dev, columns), 'obs',...  21.6 us
    all_to_all x1, waiting for transfers between devices, shards(): lax.all_to_all(jnp.broadcast_to(own_source[None], (groups, panels_dev, co...  14.4 us
    reduce_sum x2, other arithmetic, kernel_block(): real_part = jnp.sum(weight_real * amp_real + weight_imag * amp_imag, axis=1)  7.48 us
    all_to_all x1, starting transfers between devices, shards(): lax.all_to_all(jnp.broadcast_to(own_source[None], (groups, panels_dev, co...  4.1 us
    while x18, local copies, waits for them, and re-layouts  2.8 us
    ppermute x1, waiting for transfers between devices, shards(): band_total = energy + lax.ppermute(energy, 'freq', [(0, 1), (1, 0)])  2.02 us
    while x12, other arithmetic  1.71 us
    ppermute x1, starting transfers between devices, shards(): band_total = energy + lax.ppermute(energy, 'freq', [(0, 1), (1, 0)])  1.58 us
  transfers between devices with their start and end apart: 2, of which 2 were waited for; matrix products, arithmetic and copies ran while one was open for 0% of the time, Pallas kernels for 0%

commit v1 on v0

--- a/solution.py
+++ b/solution.py
@@ -6,6 +6,29 @@
 
 wave_step = 0.1
 reference_radius = 10.0
+
+
+def cut_along(x, dim, length):
+    shape = x.shape
+    blocks = x.reshape(*shape[:dim], length, shape[dim] // length, *shape[dim + 1 :])
+    return jnp.moveaxis(blocks, dim, 0)
+
+
+def in_order(blocks, dim):
+    blocks = jnp.moveaxis(blocks, 0, dim)
+    shape = blocks.shape
+    return blocks.reshape(*shape[:dim], shape[dim] * shape[dim + 1], *shape[dim + 2 :])
+
+
+def swapped_with_each(x, axis, split_dim, concat_dim):
+    peers, place = (lax.axis_size(axis), lax.axis_index(axis))
+    parts = cut_along(x, split_dim, peers)
+    outs = [parts[place]]
+    for step in range(1, peers):
+        sent = parts[place ^ step]
+        outs.append(lax.ppermute(sent, axis, [(i, i ^ step) for i in range(peers)]))
+    parts = jnp.stack(outs)[place ^ jnp.arange(peers)]
+    return in_order(parts, concat_dim)
 
 
 def phase_powers(distance, wave_numbers):
@@ -72,8 +95,8 @@
         local_source.reshape(groups, panels_dev, columns), "obs", 0, 0, tiled=True
     )
     own_source = jnp.sum(arrived, axis=0)
-    portion = lax.all_to_all(
-        jnp.broadcast_to(own_source[None], (groups, panels_dev, columns)), "obs", 0, 0, tiled=True
+    portion = swapped_with_each(
+        jnp.broadcast_to(own_source[None], (groups, panels_dev, columns)), "obs", 0, 0
     ).reshape(panel_total, columns)
     rows_count = portion.shape[0]
     tile_rows = math.gcd(rows_count, 256)

time: 64.6 us -> 72 us (1.11)
  starting transfers between devices: 5.68 us -> 29.4 us
  blocking collectives: 21.6 us -> 0 us
  waiting for transfers between devices: 16.5 us -> 21.1 us
  matrix products: 1.36 us -> 2.19 us
    all_to_all x1 -> x0, blocking collectives: 21.6 us -> none  [shards(): lax.all_to_all(local_source.reshape(groups, panels_dev, columns), 'obs',...]
    ppermute x0 -> x15, starting transfers between devices: none -> 20.5 us  [swapped_with_each(): outs.append(lax.ppermute(sent, axis, [(i, i ^ step) for i in range(peers)]))]
    ppermute x0 -> x15, waiting for transfers between devices: none -> 4.68 us  [swapped_with_each(): outs.append(lax.ppermute(sent, axis, [(i, i ^ step) for i in range(peers)]))]
    all_to_all x1, starting transfers between devices: 4.1 us -> 7.36 us  [shards(): lax.all_to_all(local_source.reshape(groups, panels_dev, columns), 'obs',...]
    broadcast_in_dim x1 -> x0, local copies, waits for them, and re-layouts: 0.84 us -> none  [shards(): jnp.broadcast_to(own_source[None], (groups, panels_dev, columns))]
    dot_general x1, matrix products: 1.36 us -> 2.19 us  [shards(): jnp.dot(selector, weighted, preferred_element_type=jnp.float32)]
  transfers between devices with their start and end apart: 2 -> 17, of which waited for: 2 -> 4; matrix products, arithmetic and copies ran while one was open for 0% -> 0% of each run, Pallas kernels for 0% -> 0%
where the time goes in v1:
time: 72 us; the launch traced here: 71.7 us
  starting transfers between devices  29.4 us (41%)
  waiting for transfers between devices  21.1 us (29%)
  other arithmetic  13.6 us (19%)
  local copies, waits for them, and re-layouts  4.16 us (6%)
  matrix products  2.19 us (3%)
  between operations  0.79 us (1%)
    ppermute x15, starting transfers between devices, swapped_with_each(): outs.append(lax.ppermute(sent, axis, [(i, i ^ step) for i in range(peers)]))  20.5 us
    all_to_all x1, waiting for transfers between devices, shards(): lax.all_to_all(local_source.reshape(groups, panels_dev, columns), 'obs',...  14.4 us
    reduce_sum x2, other arithmetic, kernel_block(): real_part = jnp.sum(weight_real * amp_real + weight_imag * amp_imag, axis=1)  7.48 us
    all_to_all x1, starting transfers between devices, shards(): lax.all_to_all(local_source.reshape(groups, panels_dev, columns), 'obs',...  7.36 us
    ppermute x15, waiting for transfers between devices, swapped_with_each(): outs.append(lax.ppermute(sent, axis, [(i, i ^ step) for i in range(peers)]))  4.68 us
    while x18, local copies, waits for them, and re-layouts  2.8 us
    dot_general x1, matrix products, shards(): jnp.dot(selector, weighted, preferred_element_type=jnp.float32)  2.19 us
    ppermute x1, waiting for transfers between devices, shards(): band_total = energy + lax.ppermute(energy, 'freq', [(0, 1), (1, 0)])  2.02 us
  transfers between devices with their start and end apart: 17, of which 4 were waited for; matrix products, arithmetic and copies ran while one was open for 0% of the time, Pallas kernels for 0%

profile of v1, /device:TPU:0, one launch (start us, length us, event | category | flops | bytes accessed | tf_op | source)
XLA Modules:
  0.0 71.7 jit_solution(6381374551735919344)
XLA Ops:
  0.6 0.7 broadcast_multiply_fusion.1
  1.3 0.7 add.304
  2.0 2.2 %fusion.12 = f32[512,256]{1,0:T(8,128)} fusion(s32[512]{0:T(512)S(1)} %add.304, bf16[512,256]{1,0:T(8,128)(2,1)} %param.8, f32[512]{0:T(512)} %param.9), kind=kOutput, calls=%fused_computation.84 | convolution fusion | flops 134873088 | bytes 790528 | tf_op jit(solution)/shard_map/dot_general | solution.py:88
  4.2 7.4 %all-to-all-start = ((f32[16,32,256]{2,1,0:T(8,128)}), f32[16,32,256]{2,1,0:T(8,128)S(1)}, u32[]{:S(2)}, u32[]{:S(2)}) async-start(f32[16,32,256]{2,1,0:T(8,128)} %bitcast.1), calls=%async_computation | async-start | bytes 1048576 | tf_op jit(solution)/shard_map/all_to_all | solution.py:94
  11.6 14.4 %all-to-all-done = f32[16,32,256]{2,1,0:T(8,128)S(1)} async-done(((f32[16,32,256]{2,1,0:T(8,128)}), f32[16,32,256]{2,1,0:T(8,128)S(1)}, u32[]{:S(2)}, u32[]{:S(2)}) %all-to-all-start) | async-done | bytes 524320 | tf_op jit(solution)/shard_map/all_to_all | solution.py:94
  26.2 1.1 %collective-permute-start.1 = (f32[1,32,256]{2,1,0:T(8,128)S(1)}, f32[1,32,256]{2,1,0:T(8,128)S(1)}, u32[]{:S(2)}, u32[]{:S(2)}) collective-permute-start(f32[1,32,256]{2,1,0:T(8,128)S(1)} %bitcast.146), channel_id=1, source_target_pairs={{0,4},{2,6},{4,0},{6,2},{8,12},{10,14},{12,8},{14,10},{16,20},{18,... | collective-permute-start | bytes 98312 | tf_op jit(solution)/shard_map/ppermute | solution.py:29
  27.3 0.7 collective-permute-start.2
  28.0 1.3 %collective-permute-start.3 = (f32[1,32,256]{2,1,0:T(8,128)S(1)}, f32[1,32,256]{2,1,0:T(8,128)S(1)}, u32[]{:S(2)}, u32[]{:S(2)}) collective-permute-start(f32[1,32,256]{2,1,0:T(8,128)S(1)} %bitcast.148), channel_id=1, source_target_pairs={{0,8},{2,10},{4,12},{6,14},{8,0},{10,2},{12,4},{14,6},{16,24},{18,... | collective-permute-start | bytes 98312 | tf_op jit(solution)/shard_map/ppermute | solution.py:29
  29.7 2.0 %collective-permute-start.5 = (f32[1,32,256]{2,1,0:T(8,128)S(1)}, f32[1,32,256]{2,1,0:T(8,128)S(1)}, u32[]{:S(2)}, u32[]{:S(2)}) collective-permute-start(f32[1,32,256]{2,1,0:T(8,128)S(1)} %bitcast.150), channel_id=1, source_target_pairs={{0,12},{2,14},{4,8},{6,10},{8,4},{10,6},{12,0},{14,2},{16,28},{18,... | collective-permute-start | bytes 98312 | tf_op jit(solution)/shard_map/ppermute | solution.py:29
  31.7 0.7 collective-permute-start.6
  32.4 2.3 %collective-permute-start.7 = (f32[1,32,256]{2,1,0:T(8,128)S(1)}, f32[1,32,256]{2,1,0:T(8,128)S(1)}, u32[]{:S(2)}, u32[]{:S(2)}) collective-permute-start(f32[1,32,256]{2,1,0:T(8,128)S(1)} %bitcast.152), channel_id=1, source_target_pairs={{0,16},{2,18},{4,20},{6,22},{8,24},{10,26},{12,28},{14,30},{16,0},... | collective-permute-start | bytes 98312 | tf_op jit(solution)/shard_map/ppermute | solution.py:29
  35.0 1.8 %collective-permute-start.9 = (f32[1,32,256]{2,1,0:T(8,128)S(1)}, f32[1,32,256]{2,1,0:T(8,128)S(1)}, u32[]{:S(2)}, u32[]{:S(2)}) collective-permute-start(f32[1,32,256]{2,1,0:T(8,128)S(1)} %bitcast.154), channel_id=1, source_target_pairs={{0,20},{2,22},{4,16},{6,18},{8,28},{10,30},{12,24},{14,26},{16,4},... | collective-permute-start | bytes 98312 | tf_op jit(solution)/shard_map/ppermute | solution.py:29
  36.8 1.8 %collective-permute-start.10 = (f32[1,32,256]{2,1,0:T(8,128)S(1)}, f32[1,32,256]{2,1,0:T(8,128)S(1)}, u32[]{:S(2)}, u32[]{:S(2)}) collective-permute-start(f32[1,32,256]{2,1,0:T(8,128)S(1)} %bitcast.155), channel_id=1, source_target_pairs={{0,22},{2,20},{4,18},{6,16},{8,30},{10,28},{12,26},{14,24},{16,6},... | collective-permute-start | bytes 98312 | tf_op jit(solution)/shard_map/ppermute | solution.py:29
  38.6 1.7 %collective-permute-start.11 = (f32[1,32,256]{2,1,0:T(8,128)S(1)}, f32[1,32,256]{2,1,0:T(8,128)S(1)}, u32[]{:S(2)}, u32[]{:S(2)}) collective-permute-start(f32[1,32,256]{2,1,0:T(8,128)S(1)} %bitcast.156), channel_id=1, source_target_pairs={{0,24},{2,26},{4,28},{6,30},{8,16},{10,18},{12,20},{14,22},{16,8},... | collective-permute-start | bytes 98312 | tf_op jit(solution)/shard_map/ppermute | solution.py:29
  40.4 1.8 %collective-permute-start.12 = (f32[1,32,256]{2,1,0:T(8,128)S(1)}, f32[1,32,256]{2,1,0:T(8,128)S(1)}, u32[]{:S(2)}, u32[]{:S(2)}) collective-permute-start(f32[1,32,256]{2,1,0:T(8,128)S(1)} %bitcast.157), channel_id=1, source_target_pairs={{0,26},{2,24},{4,30},{6,28},{8,18},{10,16},{12,22},{14,20},{16,10}... | collective-permute-start | bytes 98312 | tf_op jit(solution)/shard_map/ppermute | solution.py:29
  42.2 2.9 %collective-permute-start.13 = (f32[1,32,256]{2,1,0:T(8,128)S(1)}, f32[1,32,256]{2,1,0:T(8,128)S(1)}, u32[]{:S(2)}, u32[]{:S(2)}) collective-permute-start(f32[1,32,256]{2,1,0:T(8,128)S(1)} %bitcast.158), channel_id=1, source_target_pairs={{0,28},{2,30},{4,24},{6,26},{8,20},{10,22},{12,16},{14,18},{16,12}... | collective-permute-start | bytes 98312 | tf_op jit(solution)/shard_map/ppermute | solution.py:29
  45.1 1.6 %collective-permute-start.14 = (f32[1,32,256]{2,1,0:T(8,128)S(1)}, f32[1,32,256]{2,1,0:T(8,128)S(1)}, u32[]{:S(2)}, u32[]{:S(2)}) collective-permute-start(f32[1,32,256]{2,1,0:T(8,128)S(1)} %bitcast.159), channel_id=1, source_target_pairs={{0,30},{2,28},{4,26},{6,24},{8,22},{10,20},{12,18},{14,16},{16,14}... | collective-permute-start | bytes 98312 | tf_op jit(solution)/shard_map/ppermute | solution.py:29
  46.7 2.1 %collective-permute-done.13 = f32[1,32,256]{2,1,0:T(8,128)S(1)} collective-permute-done((f32[1,32,256]{2,1,0:T(8,128)S(1)}, f32[1,32,256]{2,1,0:T(8,128)S(1)}, u32[]{:S(2)}, u32[]{:S(2)}) %collective-permute-start.13) | collective-permute-done | bytes 32800 | tf_op jit(solution)/shard_map/ppermute | solution.py:29
  48.8 2.6 %collective-permute-done.14 = f32[1,32,256]{2,1,0:T(8,128)S(1)} collective-permute-done((f32[1,32,256]{2,1,0:T(8,128)S(1)}, f32[1,32,256]{2,1,0:T(8,128)S(1)}, u32[]{:S(2)}, u32[]{:S(2)}) %collective-permute-start.14) | collective-permute-done | bytes 32800 | tf_op jit(solution)/shard_map/ppermute | solution.py:29
  51.4 0.6 gather_fusion
  52.0 15.5 %while.14 = (s32[]{:T(128)}, f32[32,2,64]{2,0,1:T(8,128)S(1)}, f32[32]{0:T(128)S(1)}, f32[3,64]{1,0:T(4,128)S(1)}, f32[3,512]{1,0:T(4,128)S(1)}, /*index=5*/f32[...) while((s32[]{:T(128)}, f32[32,2,64]{2,0,1:T(8,128)S(1)}, f32[32]{0:T(128)S(1)}, ...), condition=%wide.region_4.0_spmd.clone, body=%wide.region_1.0_spmd.clone.sunk | while | flops 22880256 | bytes 33503556 | solution.py:111
  52.1 0.6 subtract_bitcast_fusion.2
  52.7 0.5 constant_dynamic-update-slice_fusion.41
  54.1 1.3 %copy-done = f32[32,256,64]{1,2,0:T(8,128)} copy-done((f32[32,256,64]{1,2,0:T(8,128)}, f32[32,256,64]{1,2,0:T(8,128)S(1)}, u32[]{:S(2)}) %copy-start) | copy-done | bytes 2097176 | tf_op jit(solution)/shard_map/while
  56.0 3.7 %add_reduce_fusion.2 = (f32[32,64]{1,0:T(8,128)S(1)}, f32[32,64]{1,0:T(8,128)S(1)}) fusion(f32[32,256,64]{1,2,0:T(8,128)S(1)} %get-tuple-element.339, f32[32,256,64]{1,2,0:T(8,128)} %copy-done, f32[32,256]{1,0:T(8,128)S(1)} %get-tuple-element.343, f32[32,256]{1,0:T(8,128)S(1)} %get-tuple-element.344, f32[32,256]{1,0:T(8,128)S(1)} %get-tuple-element.347, ...), kind=kLoop, calls=%fused_computation.2.clone.1 | loop fusion | flops 14675968 | bytes 4735104 | tf_op jit(solution)/shard_map/while/body/eval_jaxpr/reduce_sum | solution.py:71
  59.9 0.6 subtract_bitcast_fusion.2
  60.5 0.5 constant_dynamic-update-slice_fusion.41
  61.8 1.3 %copy-done = f32[32,256,64]{1,2,0:T(8,128)} copy-done((f32[32,256,64]{1,2,0:T(8,128)}, f32[32,256,64]{1,2,0:T(8,128)S(1)}, u32[]{:S(2)}) %copy-start) | copy-done | bytes 2097176 | tf_op jit(solution)/shard_map/while
  63.7 3.7 %add_reduce_fusion.2 = (f32[32,64]{1,0:T(8,128)S(1)}, f32[32,64]{1,0:T(8,128)S(1)}) fusion(f32[32,256,64]{1,2,0:T(8,128)S(1)} %get-tuple-element.339, f32[32,256,64]{1,2,0:T(8,128)} %copy-done, f32[32,256]{1,0:T(8,128)S(1)} %get-tuple-element.343, f32[32,256]{1,0:T(8,128)S(1)} %get-tuple-element.344, f32[32,256]{1,0:T(8,128)S(1)} %get-tuple-element.347, ...), kind=kLoop, calls=%fused_computation.2.clone.1 | loop fusion | flops 14675968 | bytes 4735104 | tf_op jit(solution)/shard_map/while/body/eval_jaxpr/reduce_sum | solution.py:71
  67.6 1.6 %collective-permute-start.15 = (f32[64]{0:T(128)S(1)}, f32[64]{0:T(128)S(1)}, u32[]{:S(2)}, u32[]{:S(2)}) collective-permute-start(f32[64]{0:T(128)S(1)} %fusion.16), channel_id=1, source_target_pairs={{0,1},{1,0},{2,3},{3,2},{4,5},{5,4},{6,7},{7,6},{8,9},{9,8},{10,11... | collective-permute-start | bytes 776 | tf_op jit(solution)/shard_map/ppermute | solution.py:115
  69.2 2.0 %collective-permute-done.15 = f32[64]{0:T(128)S(1)} collective-permute-done((f32[64]{0:T(128)S(1)}, f32[64]{0:T(128)S(1)}, u32[]{:S(2)}, u32[]{:S(2)}) %collective-permute-start.15) | collective-permute-done | bytes 288 | tf_op jit(solution)/shard_map/ppermute | solution.py:115
  71.2 0.5 add_log_fusion
  (95 shorter events, 3.8 us)
Async XLA Ops:
  2.0 50.0 %copy-start.1 = (f32[3,64]{1,0:T(4,128)S(1)}, f32[3,64]{1,0:T(4,128)}, u32[]{:S(2)}) copy-start(f32[3,64]{1,0:T(4,128)} %param.13) | copy-start | bytes 2308
  2.0 50.0 %copy-start.3 = (f32[3,512]{1,0:T(4,128)S(1)}, f32[3,512]{1,0:T(4,128)}, u32[]{:S(2)}) copy-start(f32[3,512]{1,0:T(4,128)} %param.12) | copy-start | bytes 18436
  4.2 21.8 %all-to-all-start = ((f32[16,32,256]{2,1,0:T(8,128)}), f32[16,32,256]{2,1,0:T(8,128)S(1)}, u32[]{:S(2)}, u32[]{:S(2)}) async-start(f32[16,32,256]{2,1,0:T(8,128)} %bitcast.1), calls=%async_computation | async-start | bytes 1048576 | tf_op jit(solution)/shard_map/all_to_all | solution.py:94
  26.1 3.7 %collective-permute-start = (f32[1,32,256]{2,1,0:T(8,128)S(1)}, f32[1,32,256]{2,1,0:T(8,128)S(1)}, u32[]{:S(2)}, u32[]{:S(2)}) collective-permute-start(f32[1,32,256]{2,1,0:T(8,128)S(1)} %bitcast.145), channel_id=1, source_target_pairs={{0,2},{2,0},{4,6},{6,4},{8,10},{10,8},{12,14},{14,12},{16,18},{18,... | collective-permute-start | bytes 98312 | tf_op jit(solution)/shard_map/ppermute | solution.py:29
  26.2 5.6 %collective-permute-start.1 = (f32[1,32,256]{2,1,0:T(8,128)S(1)}, f32[1,32,256]{2,1,0:T(8,128)S(1)}, u32[]{:S(2)}, u32[]{:S(2)}) collective-permute-start(f32[1,32,256]{2,1,0:T(8,128)S(1)} %bitcast.146), channel_id=1, source_target_pairs={{0,4},{2,6},{4,0},{6,2},{8,12},{10,14},{12,8},{14,10},{16,20},{18,... | collective-permute-start | bytes 98312 | tf_op jit(solution)/shard_map/ppermute | solution.py:29
  27.3 5.1 %collective-permute-start.2 = (f32[1,32,256]{2,1,0:T(8,128)S(1)}, f32[1,32,256]{2,1,0:T(8,128)S(1)}, u32[]{:S(2)}, u32[]{:S(2)}) collective-permute-start(f32[1,32,256]{2,1,0:T(8,128)S(1)} %bitcast.147), channel_id=1, source_target_pairs={{0,6},{2,4},{4,2},{6,0},{8,14},{10,12},{12,10},{14,8},{16,22},{18,... | collective-permute-start | bytes 98312 | tf_op jit(solution)/shard_map/ppermute | solution.py:29
  28.0 6.7 %collective-permute-start.3 = (f32[1,32,256]{2,1,0:T(8,128)S(1)}, f32[1,32,256]{2,1,0:T(8,128)S(1)}, u32[]{:S(2)}, u32[]{:S(2)}) collective-permute-start(f32[1,32,256]{2,1,0:T(8,128)S(1)} %bitcast.148), channel_id=1, source_target_pairs={{0,8},{2,10},{4,12},{6,14},{8,0},{10,2},{12,4},{14,6},{16,24},{18,... | collective-permute-start | bytes 98312 | tf_op jit(solution)/shard_map/ppermute | solution.py:29
  29.3 5.7 %collective-permute-start.4 = (f32[1,32,256]{2,1,0:T(8,128)S(1)}, f32[1,32,256]{2,1,0:T(8,128)S(1)}, u32[]{:S(2)}, u32[]{:S(2)}) collective-permute-start(f32[1,32,256]{2,1,0:T(8,128)S(1)} %bitcast.149), channel_id=1, source_target_pairs={{0,10},{2,8},{4,14},{6,12},{8,2},{10,0},{12,6},{14,4},{16,26},{18,... | collective-permute-start | bytes 98312 | tf_op jit(solution)/shard_map/ppermute | solution.py:29
  29.7 7.1 %collective-permute-start.5 = (f32[1,32,256]{2,1,0:T(8,128)S(1)}, f32[1,32,256]{2,1,0:T(8,128)S(1)}, u32[]{:S(2)}, u32[]{:S(2)}) collective-permute-start(f32[1,32,256]{2,1,0:T(8,128)S(1)} %bitcast.150), channel_id=1, source_target_pairs={{0,12},{2,14},{4,8},{6,10},{8,4},{10,6},{12,0},{14,2},{16,28},{18,... | collective-permute-start | bytes 98312 | tf_op jit(solution)/shard_map/ppermute | solution.py:29
  31.7 6.9 %collective-permute-start.6 = (f32[1,32,256]{2,1,0:T(8,128)S(1)}, f32[1,32,256]{2,1,0:T(8,128)S(1)}, u32[]{:S(2)}, u32[]{:S(2)}) collective-permute-start(f32[1,32,256]{2,1,0:T(8,128)S(1)} %bitcast.151), channel_id=1, source_target_pairs={{0,14},{2,12},{4,10},{6,8},{8,6},{10,4},{12,2},{14,0},{16,30},{18,... | collective-permute-start | bytes 98312 | tf_op jit(solution)/shard_map/ppermute | solution.py:29
  32.4 8.0 %collective-permute-start.7 = (f32[1,32,256]{2,1,0:T(8,128)S(1)}, f32[1,32,256]{2,1,0:T(8,128)S(1)}, u32[]{:S(2)}, u32[]{:S(2)}) collective-permute-start(f32[1,32,256]{2,1,0:T(8,128)S(1)} %bitcast.152), channel_id=1, source_target_pairs={{0,16},{2,18},{4,20},{6,22},{8,24},{10,26},{12,28},{14,30},{16,0},... | collective-permute-start | bytes 98312 | tf_op jit(solution)/shard_map/ppermute | solution.py:29
  34.7 7.5 %collective-permute-start.8 = (f32[1,32,256]{2,1,0:T(8,128)S(1)}, f32[1,32,256]{2,1,0:T(8,128)S(1)}, u32[]{:S(2)}, u32[]{:S(2)}) collective-permute-start(f32[1,32,256]{2,1,0:T(8,128)S(1)} %bitcast.153), channel_id=1, source_target_pairs={{0,18},{2,16},{4,22},{6,20},{8,26},{10,24},{12,30},{14,28},{16,2},... | collective-permute-start | bytes 98312 | tf_op jit(solution)/shard_map/ppermute | solution.py:29
  35.0 10.1 %collective-permute-start.9 = (f32[1,32,256]{2,1,0:T(8,128)S(1)}, f32[1,32,256]{2,1,0:T(8,128)S(1)}, u32[]{:S(2)}, u32[]{:S(2)}) collective-permute-start(f32[1,32,256]{2,1,0:T(8,128)S(1)} %bitcast.154), channel_id=1, source_target_pairs={{0,20},{2,22},{4,16},{6,18},{8,28},{10,30},{12,24},{14,26},{16,4},... | collective-permute-start | bytes 98312 | tf_op jit(solution)/shard_map/ppermute | solution.py:29
  36.8 9.8 %collective-permute-start.10 = (f32[1,32,256]{2,1,0:T(8,128)S(1)}, f32[1,32,256]{2,1,0:T(8,128)S(1)}, u32[]{:S(2)}, u32[]{:S(2)}) collective-permute-start(f32[1,32,256]{2,1,0:T(8,128)S(1)} %bitcast.155), channel_id=1, source_target_pairs={{0,22},{2,20},{4,18},{6,16},{8,30},{10,28},{12,26},{14,24},{16,6},... | collective-permute-start | bytes 98312 | tf_op jit(solution)/shard_map/ppermute | solution.py:29
  38.6 8.0 %collective-permute-start.11 = (f32[1,32,256]{2,1,0:T(8,128)S(1)}, f32[1,32,256]{2,1,0:T(8,128)S(1)}, u32[]{:S(2)}, u32[]{:S(2)}) collective-permute-start(f32[1,32,256]{2,1,0:T(8,128)S(1)} %bitcast.156), channel_id=1, source_target_pairs={{0,24},{2,26},{4,28},{6,30},{8,16},{10,18},{12,20},{14,22},{16,8},... | collective-permute-start | bytes 98312 | tf_op jit(solution)/shard_map/ppermute | solution.py:29
  40.4 6.3 %collective-permute-start.12 = (f32[1,32,256]{2,1,0:T(8,128)S(1)}, f32[1,32,256]{2,1,0:T(8,128)S(1)}, u32[]{:S(2)}, u32[]{:S(2)}) collective-permute-start(f32[1,32,256]{2,1,0:T(8,128)S(1)} %bitcast.157), channel_id=1, source_target_pairs={{0,26},{2,24},{4,30},{6,28},{8,18},{10,16},{12,22},{14,20},{16,10}... | collective-permute-start | bytes 98312 | tf_op jit(solution)/shard_map/ppermute | solution.py:29
  42.2 6.6 %collective-permute-start.13 = (f32[1,32,256]{2,1,0:T(8,128)S(1)}, f32[1,32,256]{2,1,0:T(8,128)S(1)}, u32[]{:S(2)}, u32[]{:S(2)}) collective-permute-start(f32[1,32,256]{2,1,0:T(8,128)S(1)} %bitcast.158), channel_id=1, source_target_pairs={{0,28},{2,30},{4,24},{6,26},{8,20},{10,22},{12,16},{14,18},{16,12}... | collective-permute-start | bytes 98312 | tf_op jit(solution)/shard_map/ppermute | solution.py:29
  45.1 6.3 %collective-permute-start.14 = (f32[1,32,256]{2,1,0:T(8,128)S(1)}, f32[1,32,256]{2,1,0:T(8,128)S(1)}, u32[]{:S(2)}, u32[]{:S(2)}) collective-permute-start(f32[1,32,256]{2,1,0:T(8,128)S(1)} %bitcast.159), channel_id=1, source_target_pairs={{0,30},{2,28},{4,26},{6,24},{8,22},{10,20},{12,18},{14,16},{16,14}... | collective-permute-start | bytes 98312 | tf_op jit(solution)/shard_map/ppermute | solution.py:29
  54.1 1.3 %copy-start = (f32[32,256,64]{1,2,0:T(8,128)}, f32[32,256,64]{1,2,0:T(8,128)S(1)}, u32[]{:S(2)}) copy-start(f32[32,256,64]{1,2,0:T(8,128)S(1)} %get-tuple-element.340) | copy-start | bytes 6291460 | tf_op jit(solution)/shard_map/while
  61.8 1.3 %copy-start = (f32[32,256,64]{1,2,0:T(8,128)}, f32[32,256,64]{1,2,0:T(8,128)S(1)}, u32[]{:S(2)}) copy-start(f32[32,256,64]{1,2,0:T(8,128)S(1)} %get-tuple-element.340) | copy-start | bytes 6291460 | tf_op jit(solution)/shard_map/while
  67.5 4.2 %copy-start.2 = (f32[32,2,64]{2,1,0:T(2,128)}, f32[32,2,64]{2,1,0:T(2,128)S(1)}, u32[]{:S(2)}) copy-start(f32[32,2,64]{2,1,0:T(2,128)S(1)} %copy_multiply_fusion) | copy-start | bytes 49156
  67.6 3.6 %collective-permute-start.15 = (f32[64]{0:T(128)S(1)}, f32[64]{0:T(128)S(1)}, u32[]{:S(2)}, u32[]{:S(2)}) collective-permute-start(f32[64]{0:T(128)S(1)} %fusion.16), channel_id=1, source_target_pairs={{0,1},{1,0},{2,3},{3,2},{4,5},{5,4},{6,7},{7,6},{8,9},{9,8},{10,11... | collective-permute-start | bytes 776 | tf_op jit(solution)/shard_map/ppermute | solution.py:115
